TPU v7x, 32 devices: a whole 2x2x4 slice. The times are simulated.
32 devices in a mesh: rep: 2 (over y), tp: 8 (over z, x), sub: 2 (over core).
Axes of the slice: x: 2, y: 2, z: 4, core: 2. Of those that a mesh axis runs over, the one named last changes fastest.
Arguments:
- queries: bfloat16 [2, 16, 16384], P(None, ('rep', 'sub'), 'tp'), parts along dimension 1, may hold values from -53 to 53
- prefix_kv: bfloat16 [2, 16384, 1024], P(None, ('rep', 'tp')), parts along dimension 1, may hold values from -6 to 6
- tail_kv: bfloat16 [2, 16, 1024, 1024], P(None, ('rep', 'sub'), 'tp'), parts along dimension 1, may hold values from -6 to 6
- tail_lengths: int32 [16], P(('rep', 'sub')), parts along dimension 0, may hold values from 1 to 1024, as said below
- fresh_kv: bfloat16 [2, 2, 16, 1024], P(None, None, ('rep', 'sub')), parts along dimension 2, may hold values from -6 to 6
- out_weight: bfloat16 [16384, 16384], P('tp', 'sub'), may hold values from -0.5 to 0.5
- scale_in: int32 [128], replicated, may hold values from 9 to 14
- scale_out: int32 [128], replicated, may hold values from 5 to 10
- residual: bfloat16 [2, 16, 16384], P(None, 'rep', 'sub'), parts along dimension 1, may hold values from -1.5 to 1.5
Outputs:
- hidden: bfloat16 [2, 16, 16384], P(None, 'rep', 'sub'), parts along dimension 1
There are 2 independent parts, one for each index of `rep`. A program takes and returns all parts, laid end to end along the dimension named above; an argument that names none is the same for every part. Nothing has to cross between parts.
Inputs may be any that keep to these rules, and one draw needn't show every extreme that they name: `tail_lengths`: some sample's tail reaches 1024 tokens.
All inputs are finite; a program needn't handle non-finite values.
Results may differ from a plain program's by a relative error of at most 0.0065.
Values may be sent and summed in bfloat16 or wider, within the bound.
No kernel may reach another device: no remote copies, remote signals or barrier semaphores. Data moves between devices by JAX's collectives and lax.ppermute only.
A program may use at most 192 MiB of HBM per device.

v0:
```python
import math
import jax
import jax.numpy as jnp
from jax import lax
from jax.sharding import PartitionSpec as P

DH = 128
NEG_FILL = -1e30


def per_device(
    queries, prefix_kv, tail_kv, tail_lengths, fresh_kv, out_weight, scale_in, scale_out, residual
):
    steps_n, rows_dev, width_dev = queries.shape
    heads_dev = width_dev // DH
    tp_count = lax.axis_size("tp")
    tp_rank = lax.axis_index("tp")
    sub_rank = lax.axis_index("sub")
    kv_heads = prefix_kv.shape[2] // DH
    copies = tp_count // kv_heads
    kv_group = tp_rank // copies
    prefix_dev = prefix_kv.shape[1]
    tail_dev = tail_kv.shape[2]
    score_scale = 1.0 / math.sqrt(DH)
    own_query = queries.reshape(steps_n, rows_dev, heads_dev, DH)
    own_fresh = lax.dynamic_slice_in_dim(fresh_kv, kv_group * DH, DH, 3)
    fresh_live = jnp.arange(steps_n)[None, :] <= jnp.arange(steps_n)[:, None]
    own_fresh_scores = (
        jnp.einsum("sbhd,ubd->sbhu", own_query, own_fresh[0], preferred_element_type=jnp.float32)
        * score_scale
    )
    own_fresh_scores = jnp.where(fresh_live[:, None, None, :], own_fresh_scores, NEG_FILL)
    spread_prompt = jnp.repeat(
        prefix_kv.reshape(2, prefix_dev, kv_heads, DH), copies, axis=2
    ).reshape(2, prefix_dev, tp_count * DH)
    spread_tail = jnp.repeat(
        tail_kv.reshape(2 * rows_dev, tail_dev, kv_heads, DH), copies, axis=2
    ).reshape(2 * rows_dev, tail_dev, tp_count * DH)
    moved_prompt, moved_tail = (
        lax.all_to_all(spread_prompt, "tp", split_axis=2, concat_axis=1, tiled=True),
        lax.all_to_all(spread_tail, "tp", split_axis=2, concat_axis=1, tiled=True),
    )
    tail_full = moved_tail.reshape(2, rows_dev, tail_dev * tp_count, DH)
    prompt_scores = (
        jnp.einsum("sbhd,pd->sbhp", own_query, moved_prompt[0], preferred_element_type=jnp.float32)
        * score_scale
    )
    tail_scores = (
        jnp.einsum("sbhd,btd->sbht", own_query, tail_full[0], preferred_element_type=jnp.float32)
        * score_scale
    )
    tail_live = jnp.arange(tail_dev * tp_count)[None, :] < tail_lengths[:, None]
    tail_scores = jnp.where(tail_live[None, :, None, :], tail_scores, NEG_FILL)
    peak = jnp.maximum(
        jnp.maximum(prompt_scores.max(-1), tail_scores.max(-1)), own_fresh_scores.max(-1)
    )
    prompt_weights = jnp.exp(prompt_scores - peak[..., None])
    tail_weights = jnp.exp(tail_scores - peak[..., None])
    fresh_weights = jnp.exp(own_fresh_scores - peak[..., None])
    mass = prompt_weights.sum(-1) + tail_weights.sum(-1) + fresh_weights.sum(-1)
    numer = jnp.einsum(
        "sbhp,pd->sbhd",
        prompt_weights.astype(jnp.bfloat16),
        moved_prompt[1],
        preferred_element_type=jnp.float32,
    )
    numer = numer + jnp.einsum(
        "sbht,btd->sbhd",
        tail_weights.astype(jnp.bfloat16),
        tail_full[1],
        preferred_element_type=jnp.float32,
    )
    numer = numer + jnp.einsum(
        "sbhu,ubd->sbhd",
        fresh_weights.astype(jnp.bfloat16),
        own_fresh[1],
        preferred_element_type=jnp.float32,
    )
    attended = (numer / mass[..., None]).astype(jnp.bfloat16).reshape(steps_n, rows_dev, width_dev)
    gathered = lax.all_gather(attended, "sub", axis=1, tiled=True)
    samples = gathered.shape[1]
    local_width = out_weight.shape[1]
    head_rows_in = gathered.reshape(steps_n * samples, heads_dev, DH)
    head_weights = out_weight.reshape(heads_dev, DH, local_width)
    scale_a = jnp.repeat(jnp.exp2(-scale_in.astype(jnp.float32)), 128)
    scale_b = jnp.repeat(jnp.exp2(-scale_out.astype(jnp.float32)), 128)
    local_a = lax.dynamic_slice_in_dim(scale_a, sub_rank * local_width, local_width, 0)
    local_b = lax.dynamic_slice_in_dim(scale_b, sub_rank * local_width, local_width, 0)
    per_head_term = jnp.einsum(
        "rhd,hdf->rhf", head_rows_in, head_weights, preferred_element_type=jnp.float32
    )
    clipped = jnp.clip(per_head_term / local_a[None, None, :], -127.0, 127.0).sum(1)
    summed = lax.psum_scatter(clipped, "tp", scatter_dimension=1, tiled=True)
    piece_cols = local_width // tp_count
    piece_start = sub_rank * local_width + tp_rank * piece_cols
    piece_a = lax.dynamic_slice_in_dim(scale_a, piece_start, piece_cols, 0)
    piece_b = lax.dynamic_slice_in_dim(scale_b, piece_start, piece_cols, 0)
    levels = jnp.clip(summed * piece_a / piece_b, -127.0, 127.0).astype(jnp.bfloat16)
    all_levels = lax.all_gather(levels, "tp", axis=1, tiled=True)
    restored = all_levels.astype(jnp.float32) * local_b
    hidden = residual.reshape(steps_n * samples, local_width).astype(jnp.float32) + restored
    return hidden.astype(jnp.bfloat16).reshape(steps_n, samples, local_width)


def solution(mesh):
    return jax.shard_map(
        per_device,
        mesh=mesh,
        in_specs=(
            P(None, ("rep", "sub"), "tp"),
            P(None, ("rep", "tp"), None),
            P(None, ("rep", "sub"), "tp", None),
            P(("rep", "sub")),
            P(None, None, ("rep", "sub"), None),
            P("tp", "sub"),
            P(),
            P(),
            P(None, "rep", "sub"),
        ),
        out_specs=P(None, "rep", "sub"),
        check_vma=False,
    )
```

profile of v0, /device:TPU:0, one launch (start us, length us, event | category | flops | bytes accessed | tf_op | source)
XLA Modules:
  0.0 296.8 jit_solution(12583703444207786706)
XLA Ops:
  6.5 4.3 %copy.48 = bf16[2,4,128,1024]{2,1,0,3:T(4,128)(2,1)} copy(bf16[2,4,128,1024]{3,2,1,0:T(8,128)(2,1)} %param.11) | data formatting | bytes 4194304 | tf_op args[2]
  10.8 7.3 %all-to-all-start.1 = ((bf16[8,128,1024]{1,0,2:T(8,128)(2,1)}), bf16[8,128,1024]{1,0,2:T(8,128)(2,1)S(1)}, u32[]{:S(2)}, u32[]{:S(2)}) async-start(bf16[8,128,1024]{1,0,2:T(8,128)(2,1)} %bitcast.78), calls=%async_computation.1 | async-start | bytes 4194304 | tf_op jit(solution)/shard_map/all_to_all | solution.py:41
  18.1 11.3 %copy.46 = bf16[2,1024,1024]{1,0,2:T(2,128)(2,1)} copy(bf16[2,1024,1024]{2,1,0:T(8,128)(2,1)} %param.10) | data formatting | bytes 8388608 | tf_op args[1]
  29.4 36.9 %all-to-all-done.1 = bf16[8,128,1024]{1,0,2:T(8,128)(2,1)S(1)} async-done(((bf16[8,128,1024]{1,0,2:T(8,128)(2,1)}), bf16[8,128,1024]{1,0,2:T(8,128)(2,1)S(1)}, u32[]{:S(2)}, u32[]{:S(2)}) %all-to-all-start.1) | async-done | bytes 2097184 | tf_op jit(solution)/shard_map/all_to_all | solution.py:41
  66.3 4.5 %all-to-all-start = ((bf16[2,1024,1024]{1,0,2:T(2,128)(2,1)}), bf16[2,1024,1024]{1,0,2:T(2,128)(2,1)}, u32[]{:S(2)}, u32[]{:S(2)}) async-start(bf16[2,1024,1024]{1,0,2:T(2,128)(2,1)} %copy.46), calls=%async_computation | async-start | bytes 8388608 | tf_op jit(solution)/shard_map/all_to_all | solution.py:40
  70.9 0.0 reduce-scatter.2.cloned.1.call-start
  71.0 0.1 broadcast_bitcast_fusion.1
  71.1 0.7 constant_dynamic-slice_fusion.1
  71.8 0.1 iota_compare_fusion
  71.9 0.2 fusion.28
  72.1 0.3 copy.49
  72.4 0.1 fusion.27
  72.5 0.7 copy.57
  73.2 0.7 copy.50
  73.9 0.5 fusion.30
  74.4 89.0 %all-to-all-done = bf16[2,1024,1024]{1,0,2:T(2,128)(2,1)} async-done(((bf16[2,1024,1024]{1,0,2:T(2,128)(2,1)}), bf16[2,1024,1024]{1,0,2:T(2,128)(2,1)}, u32[]{:S(2)}, u32[]{:S(2)}) %all-to-all-start) | async-done | bytes 4194336 | tf_op jit(solution)/shard_map/all_to_all | solution.py:40
  163.4 11.2 %copy.47 = bf16[2,1024,8,128]{3,1,2,0:T(8,128)(2,1)} copy(bf16[2,1024,8,128]{1,0,3,2:T(2,128)(2,1)} %bitcast.1) | data formatting | bytes 8388608 | tf_op jit(solution)/shard_map/all_to_all | solution.py:40
  174.6 2.5 fusion.26
  177.2 0.8 fusion.29
  178.0 0.8 fusion.1
  178.8 0.9 fusion.3
  179.7 0.2 fusion.16
  179.9 0.3 fusion.11
  180.2 0.2 fusion.12
  180.5 1.9 all_gather.6
  182.4 13.7 %fusion.6 = f32[16,8192]{1,0:T(8,128)} fusion(f32[8192]{0:T(1024)S(1)} %dynamic-slice-done, bf16[16,128,8192]{2,1,0:T(8,128)(2,1)} %bitcast.86, bf16[16,16,128]{2,1,0:T(8,128)(2,1)S(1)} %bitcast.85), kind=kOutput, calls=%fused_computation.8 | convolution fusion | flops 543031296 | bytes 34177024 | tf_op jit(solution)/shard_map/rhd,hdf->rhf/dot_general | solution.py:89
  196.2 0.0 reduce-scatter.2.cloned.1.call-update
  196.2 0.1 broadcast_bitcast_fusion
  196.4 61.0 %reduce-scatter.2.cloned.1.call-done = f32[16,1024]{1,0:T(8,128)} async-done(((f32[16,8192]{1,0:T(8,128)}), f32[16,1024]{1,0:T(8,128)}) %reduce-scatter.2.cloned.1.call-update) | async-done | bytes 65552 | tf_op jit(solution)/shard_map/reduce_scatter | solution.py:93
  257.4 0.9 clamp_convert_fusion
  258.2 30.9 %all_gather.7 = bf16[16,8192]{1,0:T(8,128)(2,1)S(1)} all-gather(bf16[16,1024]{1,0:T(8,128)(2,1)S(1)} %clamp_convert_fusion), channel_id=1, replica_groups=mesh['rep'=2,'tp'=8,'sub'=2] {'tp'}, dimensions={1}, use_global_device_ids=true | all-gather | bytes 294912 | tf_op jit(solution)/shard_map/all_gather | solution.py:99
  289.2 0.8 fusion.18
  (31 shorter events, 0.2 us)
Async XLA Ops:
  10.8 55.5 %all-to-all-start.1 = ((bf16[8,128,1024]{1,0,2:T(8,128)(2,1)}), bf16[8,128,1024]{1,0,2:T(8,128)(2,1)S(1)}, u32[]{:S(2)}, u32[]{:S(2)}) async-start(bf16[8,128,1024]{1,0,2:T(8,128)(2,1)} %bitcast.78), calls=%async_computation.1 | async-start | bytes 4194304 | tf_op jit(solution)/shard_map/all_to_all | solution.py:41
  29.4 41.5 %copy-start.3 = (bf16[2,4,2048]{2,1,0:T(4,128)(2,1)S(1)}, bf16[2,4,2048]{2,1,0:T(4,128)(2,1)}, u32[]{:S(2)}) copy-start(bf16[2,4,2048]{2,1,0:T(4,128)(2,1)} %param.9) | copy-start | bytes 98308
  29.4 41.6 %copy-start.5 = (s32[128]{0:T(128)S(1)}, s32[128]{0:T(128)}, u32[]{:S(2)}) copy-start(s32[128]{0:T(128)} %param.15) | copy-start | bytes 1540
  29.4 42.4 %copy-start.4 = (s32[4]{0:T(128)S(1)}, s32[4]{0:T(128)}, u32[]{:S(2)}) copy-start(s32[4]{0:T(128)} %param.12) | copy-start | bytes 52
  66.3 97.1 %all-to-all-start = ((bf16[2,1024,1024]{1,0,2:T(2,128)(2,1)}), bf16[2,1024,1024]{1,0,2:T(2,128)(2,1)}, u32[]{:S(2)}, u32[]{:S(2)}) async-start(bf16[2,1024,1024]{1,0,2:T(2,128)(2,1)} %copy.46), calls=%async_computation | async-start | bytes 8388608 | tf_op jit(solution)/shard_map/all_to_all | solution.py:40
  70.9 186.5 %reduce-scatter.2.cloned.1.call-start = ((), (), s32[]{:S(2)}) async-start(), calls=%async_computation.3 | async-start | bytes 589824 | tf_op jit(solution)/shard_map/reduce_scatter | solution.py:93
  71.1 1.5 copy-start.1
  178.8 3.6 %dynamic-slice-start = ((f32[16384]{0:T(1024)}, s32[]{:T(128)}), f32[8192]{0:T(1024)S(1)}, s32[]{:S(2)}) async-start(f32[16384]{0:T(1024)} %copy-done.1, s32[]{:T(128)} %select_n.29), calls=%async_computation.4 | async-start | bytes 66048 | tf_op jit(solution)/shard_map/dynamic_slice | solution.py:87
  182.4 13.8 %copy-start.6 = (s32[128]{0:T(128)S(1)}, s32[128]{0:T(128)}, u32[]{:S(2)}) copy-start(s32[128]{0:T(128)} %param.16) | copy-start | bytes 1540
  182.4 13.9 %copy-start.2 = (f32[16384]{0:T(1024)S(1)}, f32[16384]{0:T(1024)}, u32[]{:S(2)}) copy-start(f32[16384]{0:T(1024)} %copy-done.1) | copy-start | bytes 196612
  182.4 106.7 %copy-start = (bf16[2,8,8192]{2,1,0:T(8,128)(2,1)S(1)}, bf16[2,8,8192]{2,1,0:T(8,128)(2,1)}, u32[]{:S(2)}) copy-start(bf16[2,8,8192]{2,1,0:T(8,128)(2,1)} %param.17) | copy-start | bytes 786436
Sparse Core Ops, SparseCore 0:
  196.3 61.0 reduce-scatter.1
where the time goes:
time: 298 us; the launch traced here: 297 us
  waiting for transfers between devices  187 us (63%)
  blocking collectives  32.8 us (11%)
  local copies, waits for them, and re-layouts  32.1 us (11%)
  matrix products  16.6 us (6%)
  between operations  13.7 us (5%)
  starting transfers between devices  11.8 us (4%)
    all_to_all x1, waiting for transfers between devices, per_device(): lax.all_to_all(spread_prompt, 'tp', split_axis=2, concat_axis=1, tiled=True)  89 us
    reduce_scatter x1, waiting for transfers between devices, per_device(): summed = lax.psum_scatter(clipped, 'tp', scatter_dimension=1, tiled=True)  61 us
    all_to_all x1, waiting for transfers between devices, per_device(): lax.all_to_all(spread_tail, 'tp', split_axis=2, concat_axis=1, tiled=True)  36.9 us
    all_gather x1, blocking collectives, per_device(): all_levels = lax.all_gather(levels, 'tp', axis=1, tiled=True)  30.9 us
    unnamed x17, local copies, waits for them, and re-layouts  15.7 us
    dot_general x1, matrix products, per_device(): jnp.einsum('rhd,hdf->rhf', head_rows_in, head_weights, preferred_element_...  13.7 us
    all_to_all x1, local copies, waits for them, and re-layouts, per_device(): lax.all_to_all(spread_prompt, 'tp', split_axis=2, concat_axis=1, tiled=True)  11.2 us
    all_to_all x1, starting transfers between devices, per_device(): lax.all_to_all(spread_tail, 'tp', split_axis=2, concat_axis=1, tiled=True)  7.25 us
  transfers between devices with their start and end apart: 3, of which 3 were waited for; matrix products, arithmetic and copies ran while one was open for 5% of the time, Pallas kernels for 0%

commit v1 on v0

--- a/solution.py
+++ b/solution.py
@@ -6,6 +6,28 @@
 
 DH = 128
 NEG_FILL = -1e30
+
+
+def in_order(blocks, dim):
+    blocks = jnp.moveaxis(blocks, 0, dim)
+    shape = blocks.shape
+    return blocks.reshape(*shape[:dim], shape[dim] * shape[dim + 1], *shape[dim + 2 :])
+
+
+def doubled(shard, axis):
+    peers = lax.axis_size(axis)
+    pieces = shard[None]
+    for level in range(peers.bit_length() - 1):
+        bit = 1 << level
+        partner_block = lax.ppermute(pieces, axis, [(i, i ^ bit) for i in range(peers)])
+        both = jnp.stack([pieces, partner_block])
+        upper = lax.axis_index(axis) >> level & 1
+        pieces = jnp.where(upper == 0, both, both[::-1]).reshape(-1, *shard.shape)
+    return pieces
+
+
+def doubled_up(x, axis, dim):
+    return in_order(doubled(x, axis), dim)
 
 
 def per_device(
@@ -96,7 +118,7 @@
     piece_a = lax.dynamic_slice_in_dim(scale_a, piece_start, piece_cols, 0)
     piece_b = lax.dynamic_slice_in_dim(scale_b, piece_start, piece_cols, 0)
     levels = jnp.clip(summed * piece_a / piece_b, -127.0, 127.0).astype(jnp.bfloat16)
-    all_levels = lax.all_gather(levels, "tp", axis=1, tiled=True)
+    all_levels = doubled_up(levels, "tp", 1)
     restored = all_levels.astype(jnp.float32) * local_b
     hidden = residual.reshape(steps_n * samples, local_width).astype(jnp.float32) + restored
     return hidden.astype(jnp.bfloat16).reshape(steps_n, samples, local_width)

time: 298 us -> 284 us (0.953)
  blocking collectives: 32.8 us -> 1.85 us
  waiting for transfers between devices: 187 us -> 199 us
  starting transfers between devices: 11.8 us -> 15.5 us
    all_gather x1 -> x0, blocking collectives: 30.9 us -> none  [per_device(): all_levels = lax.all_gather(levels, 'tp', axis=1, tiled=True)]
    ppermute x0 -> x3, waiting for transfers between devices: none -> 12.6 us  [doubled(): lax.ppermute(pieces, axis, [(i, i ^ bit) for i in range(peers)])]
    ppermute x0 -> x3, starting transfers between devices: none -> 3.61 us  [doubled(): lax.ppermute(pieces, axis, [(i, i ^ bit) for i in range(peers)])]
  transfers between devices with their start and end apart: 3 -> 6, of which waited for: 3 -> 6; matrix products, arithmetic and copies ran while one was open for 5% -> 6% of each run, Pallas kernels for 0% -> 0%
where the time goes in v1:
time: 284 us; the launch traced here: 283 us
  waiting for transfers between devices  199 us (70%)
  local copies, waits for them, and re-layouts  32.6 us (11%)
  matrix products  16.6 us (6%)
  starting transfers between devices  15.5 us (5%)
  between operations  13.7 us (5%)
  other arithmetic  3.8 us (1%)
    all_to_all x1, waiting for transfers between devices, per_device(): lax.all_to_all(spread_prompt, 'tp', split_axis=2, concat_axis=1, tiled=True)  89 us
    reduce_scatter x1, waiting for transfers between devices, per_device(): summed = lax.psum_scatter(clipped, 'tp', scatter_dimension=1, tiled=True)  61 us
    all_to_all x1, waiting for transfers between devices, per_device(): lax.all_to_all(spread_tail, 'tp', split_axis=2, concat_axis=1, tiled=True)  36.9 us
    unnamed x17, local copies, waits for them, and re-layouts  15.7 us
    dot_general x1, matrix products, per_device(): jnp.einsum('rhd,hdf->rhf', head_rows_in, head_weights, preferred_element_...  13.7 us
    ppermute x3, waiting for transfers between devices, doubled(): lax.ppermute(pieces, axis, [(i, i ^ bit) for i in range(peers)])  12.6 us
    all_to_all x1, local copies, waits for them, and re-layouts, per_device(): lax.all_to_all(spread_prompt, 'tp', split_axis=2, concat_axis=1, tiled=True)  11.2 us
    all_to_all x1, starting transfers between devices, per_device(): lax.all_to_all(spread_tail, 'tp', split_axis=2, concat_axis=1, tiled=True)  7.25 us
  transfers between devices with their start and end apart: 6, of which 6 were waited for; matrix products, arithmetic and copies ran while one was open for 6% of the time, Pallas kernels for 0%

profile of v1, /device:TPU:0, one launch (start us, length us, event | category | flops | bytes accessed | tf_op | source)
XLA Modules:
  0.0 283.5 jit_solution(3837956957820398080)
XLA Ops:
  6.5 4.3 %copy.52 = bf16[2,4,128,1024]{2,1,0,3:T(4,128)(2,1)} copy(bf16[2,4,128,1024]{3,2,1,0:T(8,128)(2,1)} %param.11) | data formatting | bytes 4194304 | tf_op args[2]
  10.8 7.3 %all-to-all-start.1 = ((bf16[8,128,1024]{1,0,2:T(8,128)(2,1)}), bf16[8,128,1024]{1,0,2:T(8,128)(2,1)S(1)}, u32[]{:S(2)}, u32[]{:S(2)}) async-start(bf16[8,128,1024]{1,0,2:T(8,128)(2,1)} %bitcast.92), calls=%async_computation.1 | async-start | bytes 4194304 | tf_op jit(solution)/shard_map/all_to_all | solution.py:63
  18.1 11.3 %copy.50 = bf16[2,1024,1024]{1,0,2:T(2,128)(2,1)} copy(bf16[2,1024,1024]{2,1,0:T(8,128)(2,1)} %param.10) | data formatting | bytes 8388608 | tf_op args[1]
  29.4 36.9 %all-to-all-done.1 = bf16[8,128,1024]{1,0,2:T(8,128)(2,1)S(1)} async-done(((bf16[8,128,1024]{1,0,2:T(8,128)(2,1)}), bf16[8,128,1024]{1,0,2:T(8,128)(2,1)S(1)}, u32[]{:S(2)}, u32[]{:S(2)}) %all-to-all-start.1) | async-done | bytes 2097184 | tf_op jit(solution)/shard_map/all_to_all | solution.py:63
  66.3 4.6 %all-to-all-start = ((bf16[2,1024,1024]{1,0,2:T(2,128)(2,1)}), bf16[2,1024,1024]{1,0,2:T(2,128)(2,1)}, u32[]{:S(2)}, u32[]{:S(2)}) async-start(bf16[2,1024,1024]{1,0,2:T(2,128)(2,1)} %copy.50), calls=%async_computation | async-start | bytes 8388608 | tf_op jit(solution)/shard_map/all_to_all | solution.py:62
  71.1 0.7 constant_dynamic-slice_fusion.1
  71.9 0.2 fusion.28
  72.1 0.3 copy.53
  72.5 0.7 copy.61
  73.2 0.7 copy.54
  73.9 0.5 fusion.30
  74.4 89.0 %all-to-all-done = bf16[2,1024,1024]{1,0,2:T(2,128)(2,1)} async-done(((bf16[2,1024,1024]{1,0,2:T(2,128)(2,1)}), bf16[2,1024,1024]{1,0,2:T(2,128)(2,1)}, u32[]{:S(2)}, u32[]{:S(2)}) %all-to-all-start) | async-done | bytes 4194336 | tf_op jit(solution)/shard_map/all_to_all | solution.py:62
  163.4 11.2 %copy.51 = bf16[2,1024,8,128]{3,1,2,0:T(8,128)(2,1)} copy(bf16[2,1024,8,128]{1,0,3,2:T(2,128)(2,1)} %bitcast) | data formatting | bytes 8388608 | tf_op jit(solution)/shard_map/all_to_all | solution.py:62
  174.6 2.5 fusion.26
  177.2 0.8 fusion.29
  178.0 0.8 fusion.1
  178.7 0.9 fusion.3
  179.7 0.2 fusion.15
  179.9 0.3 fusion.11
  180.5 1.9 all_gather.3
  182.4 13.7 %fusion.6 = f32[16,8192]{1,0:T(8,128)} fusion(f32[8192]{0:T(1024)S(1)} %dynamic-slice-done, bf16[16,128,8192]{2,1,0:T(8,128)(2,1)} %bitcast.106, bf16[16,16,128]{2,1,0:T(8,128)(2,1)S(1)} %bitcast.103), kind=kOutput, calls=%fused_computation.8 | convolution fusion | flops 543031296 | bytes 34177024 | tf_op jit(solution)/shard_map/rhd,hdf->rhf/dot_general | solution.py:111
  196.3 61.0 %reduce-scatter.2.cloned.1.call-done = f32[16,1024]{1,0:T(8,128)} async-done(((f32[16,8192]{1,0:T(8,128)}), f32[16,1024]{1,0:T(8,128)}) %reduce-scatter.2.cloned.1.call-update) | async-done | bytes 65552 | tf_op jit(solution)/shard_map/reduce_scatter | solution.py:115
  257.3 0.9 fusion.38
  258.2 1.4 collective-permute-start
  259.5 0.9 fusion.37
  260.4 1.7 collective-permute-done
  262.2 1.4 collective-permute-start.1
  263.6 4.3 %collective-permute-done.1 = bf16[2,16,1024]{2,1,0:T(8,128)(2,1)S(1)} collective-permute-done((bf16[2,16,1024]{2,1,0:T(8,128)(2,1)S(1)}, bf16[2,16,1024]{2,1,0:T(8,128)(2,1)S(1)}, u32[]{:S(2)}, u32[]{:S(2)}) %collective-permute-start.1) | collective-permute-done | bytes 65568 | tf_op jit(solution)/shard_map/ppermute | solution.py:22
  267.9 0.8 collective-permute-start.2
  268.8 6.5 %collective-permute-done.2 = bf16[4,16,1024]{2,1,0:T(8,128)(2,1)S(1)} collective-permute-done((bf16[4,16,1024]{2,1,0:T(8,128)(2,1)S(1)}, bf16[4,16,1024]{2,1,0:T(8,128)(2,1)S(1)}, u32[]{:S(2)}, u32[]{:S(2)}) %collective-permute-start.2) | collective-permute-done | bytes 131104 | tf_op jit(solution)/shard_map/ppermute | solution.py:22
  275.4 0.3 copy.109
  275.9 0.8 add_convert_fusion
  (46 shorter events, 1.1 us)
Async XLA Ops:
  10.8 55.5 %all-to-all-start.1 = ((bf16[8,128,1024]{1,0,2:T(8,128)(2,1)}), bf16[8,128,1024]{1,0,2:T(8,128)(2,1)S(1)}, u32[]{:S(2)}, u32[]{:S(2)}) async-start(bf16[8,128,1024]{1,0,2:T(8,128)(2,1)} %bitcast.92), calls=%async_computation.1 | async-start | bytes 4194304 | tf_op jit(solution)/shard_map/all_to_all | solution.py:63
  29.4 41.5 %copy-start.3 = (bf16[2,4,2048]{2,1,0:T(4,128)(2,1)S(1)}, bf16[2,4,2048]{2,1,0:T(4,128)(2,1)}, u32[]{:S(2)}) copy-start(bf16[2,4,2048]{2,1,0:T(4,128)(2,1)} %param.9) | copy-start | bytes 98308
  29.4 41.6 %copy-start.5 = (s32[128]{0:T(128)S(1)}, s32[128]{0:T(128)}, u32[]{:S(2)}) copy-start(s32[128]{0:T(128)} %param.15) | copy-start | bytes 1540
  29.4 42.4 %copy-start.4 = (s32[4]{0:T(128)S(1)}, s32[4]{0:T(128)}, u32[]{:S(2)}) copy-start(s32[4]{0:T(128)} %param.12) | copy-start | bytes 52
  66.3 97.1 %all-to-all-start = ((bf16[2,1024,1024]{1,0,2:T(2,128)(2,1)}), bf16[2,1024,1024]{1,0,2:T(2,128)(2,1)}, u32[]{:S(2)}, u32[]{:S(2)}) async-start(bf16[2,1024,1024]{1,0,2:T(2,128)(2,1)} %copy.50), calls=%async_computation | async-start | bytes 8388608 | tf_op jit(solution)/shard_map/all_to_all | solution.py:62
  70.9 186.4 %reduce-scatter.2.cloned.1.call-start = ((), (), s32[]{:S(2)}) async-start(), calls=%async_computation.3 | async-start | bytes 589824 | tf_op jit(solution)/shard_map/reduce_scatter | solution.py:115
  71.1 1.5 copy-start.1
  178.7 3.6 %dynamic-slice-start = ((f32[16384]{0:T(1024)}, s32[]{:T(128)}), f32[8192]{0:T(1024)S(1)}, s32[]{:S(2)}) async-start(f32[16384]{0:T(1024)} %copy-done.1, s32[]{:T(128)} %select_n.56), calls=%async_computation.4 | async-start | bytes 66048 | tf_op jit(solution)/shard_map/dynamic_slice | solution.py:109
  182.4 13.8 %copy-start.2 = (f32[16384]{0:T(1024)S(1)}, f32[16384]{0:T(1024)}, u32[]{:S(2)}) copy-start(f32[16384]{0:T(1024)} %copy-done.1) | copy-start | bytes 196612
  182.4 13.8 %copy-start.6 = (s32[128]{0:T(128)S(1)}, s32[128]{0:T(128)}, u32[]{:S(2)}) copy-start(s32[128]{0:T(128)} %param.16) | copy-start | bytes 1540
  196.1 79.7 %copy-start = (bf16[2,8,8192]{2,1,0:T(8,128)(2,1)S(1)}, bf16[2,8,8192]{2,1,0:T(8,128)(2,1)}, u32[]{:S(2)}) copy-start(bf16[2,8,8192]{2,1,0:T(8,128)(2,1)} %param.17) | copy-start | bytes 786436
  258.2 4.0 %collective-permute-start = (bf16[1,16,1024]{2,1,0:T(8,128)(2,1)S(1)}, bf16[1,16,1024]{2,1,0:T(8,128)(2,1)S(1)}, u32[]{:S(2)}, u32[]{:S(2)}) collective-permute-start(bf16[1,16,1024]{2,1,0:T(8,128)(2,1)S(1)} %fusion.38), channel_id=1, source_target_pairs={{0,2},{2,0},{4,6},{6,4},{8,10},{10,8},{12,14},{14,12},{1,3},{3,1},... | collective-permute-start | bytes 98312 | tf_op jit(solution)/shard_map/ppermute | solution.py:22
  262.2 5.7 %collective-permute-start.1 = (bf16[2,16,1024]{2,1,0:T(8,128)(2,1)S(1)}, bf16[2,16,1024]{2,1,0:T(8,128)(2,1)S(1)}, u32[]{:S(2)}, u32[]{:S(2)}) collective-permute-start(bf16[2,16,1024]{2,1,0:T(8,128)(2,1)S(1)} %get-tuple-element.12), channel_id=1, source_target_pairs={{0,4},{2,6},{4,0},{6,2},{8,12},{10,14},{12,8},{14,10},{1,5},{3,7},... | collective-permute-start | bytes 196616 | tf_op jit(solution)/shard_map/ppermute | solution.py:22
  267.9 7.3 %collective-permute-start.2 = (bf16[4,16,1024]{2,1,0:T(8,128)(2,1)S(1)}, bf16[4,16,1024]{2,1,0:T(8,128)(2,1)S(1)}, u32[]{:S(2)}, u32[]{:S(2)}) collective-permute-start(bf16[4,16,1024]{2,1,0:T(8,128)(2,1)S(1)} %bitcast.99), channel_id=1, source_target_pairs={{0,8},{2,10},{4,12},{6,14},{8,0},{10,2},{12,4},{14,6},{1,9},{3,11}... | collective-permute-start | bytes 393224 | tf_op jit(solution)/shard_map/ppermute | solution.py:22
Sparse Core Ops, SparseCore 0:
  196.3 60.9 reduce-scatter.1
